TPU v7x, 128 devices: a whole 4x4x4 slice. The times are simulated.
128 devices in a mesh: row: 8 (over z_hi, x), col: 16 (over z_lo, y, core).
Axes of the slice: x: 4, y: 4, z: 4 (z_hi: 2, z_lo: 2; z = z_hi * 2 + z_lo), core: 2. Of those that a mesh axis runs over, the one named last changes fastest.
Arguments:
- tokens: bfloat16 [1024, 8192], P(('row', 'col')), may hold values from -6 to 6
- gain: float32 [8192], replicated, may hold values from 0.5 to 1.5
- grad_out: bfloat16 [1024, 8192], P(('row', 'col')), may hold values from -4 to 4
- pre_gate: bfloat16 [1024, 28672], P('col', 'row'), may hold values from -6 to 6
- pre_up: bfloat16 [1024, 28672], P('col', 'row'), may hold values from -6 to 6
- gate_weight: bfloat16 [8192, 28672], P('col', 'row'), may hold values from -0.0625 to 0.0625
- up_weight: bfloat16 [8192, 28672], P('col', 'row'), may hold values from -0.0625 to 0.0625
- down_weight: bfloat16 [28672, 8192], P('row', 'col'), may hold values from -0.03125 to 0.03125
Outputs:
- grad_tokens: bfloat16 [1024, 8192], P(('row', 'col'))
- grad_gain: float32 [8192], replicated
- grad_gate: bfloat16 [8192, 28672], P('col', 'row')
- grad_up: bfloat16 [8192, 28672], P('col', 'row')
- grad_down: bfloat16 [28672, 8192], P('row', 'col')
All inputs are finite; a program needn't handle non-finite values.
Results may differ from a plain program's by a relative error of at most 0.0057.
Values may be sent and summed in bfloat16 or wider, within the bound.
No kernel may reach another device: no remote copies, remote signals or barrier semaphores. Data moves between devices by JAX's collectives and lax.ppermute only.
A program may use at most 192 MiB of HBM per device.

v0:
```python
import jax
import jax.numpy as jnp
from jax import lax
from jax.sharding import PartitionSpec as P

epsilon = 1e-05


def swiglu_grads(hidden_grad, pre_gate, pre_up):
    gate_wide = pre_gate.astype(jnp.float32)
    up_wide = pre_up.astype(jnp.float32)
    sigmoid = jax.nn.sigmoid(gate_wide)
    silu = gate_wide * sigmoid
    hidden = (silu * up_wide).astype(jnp.bfloat16)
    up_grad = (hidden_grad * silu).astype(jnp.bfloat16)
    gate_grad = (hidden_grad * up_wide * sigmoid * (1.0 + gate_wide * (1.0 - sigmoid))).astype(
        jnp.bfloat16
    )
    return (hidden, gate_grad, up_grad)


def local(tokens, gain, grad_out, pre_gate, pre_up, gate_weight, up_weight, down_weight):
    tokens_wide = tokens.astype(jnp.float32)
    inverse_rms = lax.rsqrt(jnp.mean(tokens_wide * tokens_wide, axis=1, keepdims=True) + epsilon)
    normed = tokens_wide * inverse_rms
    scaled = (normed * gain).astype(jnp.bfloat16)
    grid_input, grid_grad = (
        lax.all_to_all(scaled, "col", split_axis=1, concat_axis=0, tiled=True),
        lax.all_to_all(grad_out, "col", split_axis=1, concat_axis=0, tiled=True),
    )
    all_input, all_grad = (
        lax.all_gather(grid_input, "row", axis=0, tiled=True),
        lax.all_gather(grid_grad, "row", axis=0, tiled=True),
    )
    partial_grad = jnp.einsum(
        "td,fd->tf", all_grad, down_weight, preferred_element_type=jnp.float32
    )
    summed_grad = lax.psum(partial_grad, "col")
    hidden_piece, gate_piece, up_piece = swiglu_grads(
        summed_grad,
        lax.all_gather(pre_gate, "col", axis=0, tiled=True),
        lax.all_gather(pre_up, "col", axis=0, tiled=True),
    )
    down_total = jnp.einsum("tf,td->fd", hidden_piece, all_grad, preferred_element_type=jnp.float32)
    gate_total = jnp.einsum("td,tf->df", all_input, gate_piece, preferred_element_type=jnp.float32)
    up_total = jnp.einsum("td,tf->df", all_input, up_piece, preferred_element_type=jnp.float32)
    new_rows = jnp.einsum("tf,df->td", gate_piece, gate_weight, preferred_element_type=jnp.float32)
    new_rows = new_rows + jnp.einsum(
        "tf,df->td", up_piece, up_weight, preferred_element_type=jnp.float32
    )
    back_rows = new_rows
    results = (down_total, gate_total, up_total, back_rows)
    down_total, gate_total, up_total, back_rows = results
    grid_back = lax.psum_scatter(back_rows, "row", scatter_dimension=0, tiled=True)
    normed_grad = lax.all_to_all(grid_back, "col", split_axis=0, concat_axis=1, tiled=True)
    grad_gain = lax.psum(jnp.sum(normed_grad * normed, axis=0), ("row", "col"))
    scaled_grad = normed_grad * gain
    inner = jnp.mean(scaled_grad * normed, axis=1, keepdims=True)
    grad_tokens = (
        grad_out.astype(jnp.float32) + inverse_rms * (scaled_grad - normed * inner)
    ).astype(jnp.bfloat16)
    return (
        grad_tokens,
        grad_gain,
        gate_total.astype(jnp.bfloat16),
        up_total.astype(jnp.bfloat16),
        down_total.astype(jnp.bfloat16),
    )


def solution(mesh):
    in_specs = (
        P(("row", "col"), None),
        P(),
        P(("row", "col"), None),
        P("col", "row"),
        P("col", "row"),
        P("col", "row"),
        P("col", "row"),
        P("row", "col"),
    )
    out_specs = (P(("row", "col"), None), P(), P("col", "row"), P("col", "row"), P("row", "col"))
    return jax.shard_map(local, mesh=mesh, in_specs=in_specs, out_specs=out_specs, check_vma=False)
```

profile of v0, /device:TPU:1, one launch (start us, length us, event | category | flops | bytes accessed | tf_op | source)
XLA Modules:
  0.0 565.8 jit_solution(3937982184247556598)
XLA Ops:
  7.2 0.0 all-gather.5.cloned.1.call-start
  7.2 13.5 %all_to_all.57 = bf16[8,16,512]{2,0,1:T(8,128)(2,1)} all-to-all(bf16[8,16,512]{2,0,1:T(8,128)(2,1)} %bitcast.27), channel_id=1, replica_groups=mesh['row'=8,'col'=16] {'col'}, dimensions={1} | all-to-all | bytes 262144 | tf_op jit(solution)/shard_map/all_to_all | solution.py:29
  20.7 0.0 all-gather.5.cloned.1.call-update
  20.7 0.0 all-gather.7.cloned.1.call-start
  20.8 0.7 all-gather.7.cloned.1.call-update
  21.5 0.0 all-gather.9.cloned.1.call-start
  21.5 0.7 all-gather.9.cloned.1.call-update
  22.2 0.0 all-reduce.2.cloned.1.call-start
  22.3 43.9 %all-gather.5.cloned.1.call-done = bf16[1024,512]{1,0:T(8,128)(2,1)} async-done(((bf16[128,512]{1,0:T(8,128)(2,1)}), bf16[1024,512]{1,0:T(8,128)(2,1)}) %all-gather.5.cloned.1.call-update) | async-done | bytes 1048592 | tf_op jit(solution)/shard_map/all_gather | solution.py:33
  66.2 11.5 %fusion.26 = f32[1024,3584]{1,0:T(8,128)} fusion(bf16[1024,512]{1,0:T(8,128)(2,1)} %all-gather.5.cloned.1.call-done, bf16[3584,512]{1,0:T(8,128)(2,1)} %param.15), kind=kOutput, calls=%fused_computation.36 | convolution fusion | flops 3758096384 | bytes 19398656 | tf_op jit(solution)/shard_map/td,fd->tf/dot_general | solution.py:35
  77.7 0.0 all-reduce.2.cloned.1.call-update
  77.7 0.0 reduce-scatter.2.cloned.1.call-start
  77.8 38.1 %all-gather.7.cloned.1.call-done = bf16[1024,3584]{1,0:T(8,128)(2,1)} async-done(((bf16[64,3584]{1,0:T(8,128)(2,1)}), bf16[1024,3584]{1,0:T(8,128)(2,1)}) %all-gather.7.cloned.1.call-update) | async-done | bytes 7340048 | tf_op jit(solution)/shard_map/all_gather | solution.py:42
  115.8 49.7 %all-gather.9.cloned.1.call-done = bf16[1024,3584]{1,0:T(8,128)(2,1)} async-done(((bf16[64,3584]{1,0:T(8,128)(2,1)}), bf16[1024,3584]{1,0:T(8,128)(2,1)}) %all-gather.9.cloned.1.call-update) | async-done | bytes 7340048 | tf_op jit(solution)/shard_map/all_gather | solution.py:41
  165.6 177.7 %all-reduce.2.cloned.1.call-done = f32[1024,3584]{1,0:T(8,128)} async-done(((f32[1024,3584]{1,0:T(8,128)}), f32[1024,3584]{1,0:T(8,128)}) %all-reduce.2.cloned.1.call-update) | async-done | bytes 14680080 | tf_op jit(solution)/shard_map/psum | solution.py:38
  343.3 12.5 %multiply_convert_fusion = (bf16[1024,3584]{1,0:T(8,128)(2,1)S(1)}, bf16[1024,3584]{1,0:T(8,128)(2,1)S(1)}) fusion(f32[1024,3584]{1,0:T(8,128)} %all-reduce.2.cloned.1.call-done, bf16[1024,3584]{1,0:T(8,128)(2,1)} %all-gather.9.cloned.1.call-done, bf16[1024,3584]{1,0:T(8,128)(2,1)} %all-gather.7.cloned.1.call-done), kind=kLoop, calls=%fused_computation.13 | loop fusion | flops 55050240 | bytes 44040192 | tf_op jit(solution)/shard_map/convert_element_type | solution.py:15
  355.8 4.0 fusion.27
  359.8 2.0 copy-done.1
  361.8 5.3 convolution_add_fusion
  367.1 75.7 %reduce-scatter.2.cloned.1.call-done = f32[128,512]{1,0:T(8,128)} async-done(((f32[1024,512]{1,0:T(8,128)}), f32[128,512]{1,0:T(8,128)}) %reduce-scatter.2.cloned.1.call-update) | async-done | bytes 262160 | tf_op jit(solution)/shard_map/reduce_scatter | solution.py:54
  442.8 6.5 %all-to-all-start.1 = ((f32[16,8,512]{2,1,0:T(8,128)}), f32[16,8,512]{2,1,0:T(8,128)S(1)}, u32[]{:S(2)}, u32[]{:S(2)}) async-start(f32[16,8,512]{2,1,0:T(8,128)} %bitcast.28), calls=%async_computation.2 | async-start | bytes 524288 | tf_op jit(solution)/shard_map/all_to_all | solution.py:55
  449.3 0.2 fusion.24
  449.5 7.0 %all-to-all-done.1 = f32[16,8,512]{2,1,0:T(8,128)S(1)} async-done(((f32[16,8,512]{2,1,0:T(8,128)}), f32[16,8,512]{2,1,0:T(8,128)S(1)}, u32[]{:S(2)}, u32[]{:S(2)}) %all-to-all-start.1) | async-done | bytes 262176 | tf_op jit(solution)/shard_map/all_to_all | solution.py:55
  456.5 0.9 fusion.22
  457.5 4.0 all-to-all-start.2
  461.5 0.2 all-gather.11.cloned.1.call-start
  461.8 10.3 %fusion.10 = bf16[3584,512]{1,0:T(8,128)(2,1)} fusion(bf16[1024,512]{1,0:T(8,128)(2,1)S(1)} %copy-done.8, bf16[1024,3584]{1,0:T(8,128)(2,1)} %all-gather.7.cloned.1.call-done, bf16[1024,3584]{1,0:T(8,128)(2,1)} %all-gather.9.cloned.1.call-done), kind=kOutput, calls=%fused_computation.15 | convolution fusion | flops 3789291520 | bytes 19398656 | tf_op jit(solution)/shard_map/tf,td->fd/dot_general | solution.py:44
  472.1 0.7 copy-done.3
  472.8 67.5 %psum.15 = f32[8192]{0:T(1024)} all-reduce(f32[8192]{0:T(1024)S(1)} %get-tuple-element.5), channel_id=1, replica_groups=mesh['row'=8,'col'=16] {'row','col'}, use_global_device_ids=true, to_apply=%region_5.0 | all-reduce | flops 8192 | bytes 65536 | tf_op jit(solution)/shard_map/psum | solution.py:56
  540.3 0.8 fusion.21
  541.1 9.3 %convolution_convert_fusion = bf16[512,3584]{1,0:T(8,128)(2,1)} fusion(bf16[1024,512]{1,0:T(8,128)(2,1)} %all-gather.11.cloned.1.call-done, bf16[1024,3584]{1,0:T(8,128)(2,1)} %copy-done.1), kind=kOutput, calls=%fused_computation.16 | convolution fusion | flops 3759931392 | bytes 12058624 | tf_op jit(solution)/shard_map/td,tf->df/dot_general | solution.py:46
  550.4 8.5 %convolution_convert_fusion.1 = bf16[512,3584]{1,0:T(8,128)(2,1)} fusion(bf16[1024,512]{1,0:T(8,128)(2,1)S(1)} %copy-done.9, bf16[1024,3584]{1,0:T(8,128)(2,1)} %copy-done), kind=kOutput, calls=%fused_computation.17 | convolution fusion | flops 3759931392 | bytes 12058624 | tf_op jit(solution)/shard_map/td,tf->df/dot_general | solution.py:45
  (24 shorter events, 0.1 us)
Async XLA Ops:
  7.2 59.0 %all-gather.5.cloned.1.call-start = ((), (), s32[]{:S(2)}) async-start(), calls=%async_computation.4 | async-start | bytes 1179648 | tf_op jit(solution)/shard_map/all_gather | solution.py:33
  20.7 95.1 %all-gather.7.cloned.1.call-start = ((), (), s32[]{:S(2)}) async-start(), calls=%async_computation.6 | async-start | bytes 7798784 | tf_op jit(solution)/shard_map/all_gather | solution.py:42
  21.5 144.1 %all-gather.9.cloned.1.call-start = ((), (), s32[]{:S(2)}) async-start(), calls=%async_computation.7 | async-start | bytes 7798784 | tf_op jit(solution)/shard_map/all_gather | solution.py:41
  22.2 321.1 %all-reduce.2.cloned.1.call-start = ((), (), s32[]{:S(2)}) async-start(), calls=%async_computation.5 | async-start | bytes 29360128 | tf_op jit(solution)/shard_map/psum | solution.py:38
  77.7 365.1 %reduce-scatter.2.cloned.1.call-start = ((), (), s32[]{:S(2)}) async-start(), calls=%async_computation.8 | async-start | bytes 2359296 | tf_op jit(solution)/shard_map/reduce_scatter | solution.py:54
  343.3 12.5 %copy-start.6 = (bf16[512,3584]{1,0:T(8,128)(2,1)S(1)}, bf16[512,3584]{1,0:T(8,128)(2,1)}, u32[]{:S(2)}) copy-start(bf16[512,3584]{1,0:T(8,128)(2,1)} %param.13) | copy-start | bytes 11010052
  355.8 4.0 copy-start
  355.8 6.0 %copy-start.1 = (bf16[1024,3584]{1,0:T(8,128)(2,1)}, bf16[1024,3584]{1,0:T(8,128)(2,1)S(1)}, u32[]{:S(2)}) copy-start(bf16[1024,3584]{1,0:T(8,128)(2,1)S(1)} %get-tuple-element.7) | copy-start | bytes 22020100
  355.8 6.0 %copy-start.7 = (bf16[512,3584]{1,0:T(8,128)(2,1)S(1)}, bf16[512,3584]{1,0:T(8,128)(2,1)}, u32[]{:S(2)}) copy-start(bf16[512,3584]{1,0:T(8,128)(2,1)} %param.14) | copy-start | bytes 11010052
  361.8 87.6 %copy-start.2 = (bf16[8,8192]{1,0:T(8,128)(2,1)S(1)}, bf16[8,8192]{1,0:T(8,128)(2,1)}, u32[]{:S(2)}) copy-start(bf16[8,8192]{1,0:T(8,128)(2,1)} %param.8) | copy-start | bytes 393220
  361.8 94.8 %copy-start.5 = (f32[8192]{0:T(1024)S(1)}, f32[8192]{0:T(1024)}, u32[]{:S(2)}) copy-start(f32[8192]{0:T(1024)} %param.9) | copy-start | bytes 98308
  361.8 100.0 %copy-start.8 = (bf16[1024,512]{1,0:T(8,128)(2,1)S(1)}, bf16[1024,512]{1,0:T(8,128)(2,1)}, u32[]{:S(2)}) copy-start(bf16[1024,512]{1,0:T(8,128)(2,1)} %all-gather.5.cloned.1.call-done) | copy-start | bytes 3145732
  442.8 13.7 %all-to-all-start.1 = ((f32[16,8,512]{2,1,0:T(8,128)}), f32[16,8,512]{2,1,0:T(8,128)S(1)}, u32[]{:S(2)}, u32[]{:S(2)}) async-start(f32[16,8,512]{2,1,0:T(8,128)} %bitcast.28), calls=%async_computation.2 | async-start | bytes 524288 | tf_op jit(solution)/shard_map/all_to_all | solution.py:55
  457.5 14.6 %all-to-all-start.2 = ((bf16[8,16,512]{2,0,1:T(8,128)(2,1)}), bf16[8,16,512]{2,0,1:T(8,128)(2,1)S(1)}, u32[]{:S(2)}, u32[]{:S(2)}) async-start(bf16[8,16,512]{2,0,1:T(8,128)(2,1)} %bitcast.7), calls=%async_computation.3 | async-start | bytes 262144 | tf_op jit(solution)/shard_map/all_to_all | solution.py:28
  461.5 78.8 %copy-start.4 = (bf16[8,8192]{1,0:T(8,128)(2,1)S(1)}, bf16[8,8192]{1,0:T(8,128)(2,1)}, u32[]{:S(2)}) copy-start(bf16[8,8192]{1,0:T(8,128)(2,1)} %param.10) | copy-start | bytes 393220
  461.5 79.6 %all-gather.11.cloned.1.call-start = ((), (), s32[]{:S(2)}) async-start(), calls=%async_computation.9 | async-start | bytes 1179648 | tf_op jit(solution)/shard_map/all_gather | solution.py:32
  472.1 0.7 copy-start.3
  541.1 9.3 %copy-start.9 = (bf16[1024,512]{1,0:T(8,128)(2,1)S(1)}, bf16[1024,512]{1,0:T(8,128)(2,1)}, u32[]{:S(2)}) copy-start(bf16[1024,512]{1,0:T(8,128)(2,1)} %all-gather.11.cloned.1.call-done) | copy-start | bytes 3145732
Sparse Core Ops, SparseCore 0:
  20.8 45.2 all-gather.4
  67.9 47.9 all-gather.6
  117.5 47.9 all-gather.8
  168.0 175.2 all-reduce.1
  367.2 75.5 reduce-scatter.1
  472.9 45.2 all-gather.10
where the time goes:
time: 566 us
  waiting for transfers between devices  394 us (70%)
  blocking collectives  81 us (14%)
  matrix products  48.9 us (9%)
  other arithmetic  14.4 us (3%)
  between operations  14.2 us (3%)
  starting transfers between devices  11 us (2%)
    psum x1, waiting for transfers between devices, local(): summed_grad = lax.psum(partial_grad, 'col')  178 us
    reduce_scatter x1, waiting for transfers between devices, local(): lax.psum_scatter(back_rows, 'row', scatter_dimension=0, tiled=True)  75.7 us
    psum x1, blocking collectives, local(): grad_gain = lax.psum(jnp.sum(normed_grad * normed, axis=0), ('row', 'col'))  67.5 us
    all_gather x1, waiting for transfers between devices, local(): lax.all_gather(pre_gate, 'col', axis=0, tiled=True)  49.7 us
    all_gather x1, waiting for transfers between devices, local(): lax.all_gather(grid_grad, 'row', axis=0, tiled=True)  43.9 us
    all_gather x1, waiting for transfers between devices, local(): lax.all_gather(pre_up, 'col', axis=0, tiled=True)  38.1 us
    all_to_all x1, blocking collectives, local(): lax.all_to_all(grad_out, 'col', split_axis=1, concat_axis=0, tiled=True)  13.5 us
    convert_element_type x1, other arithmetic, swiglu_grads(): up_grad = (hidden_grad * silu).astype(jnp.bfloat16)  12.5 us
  transfers between devices with their start and end apart: 8, of which 6 were waited for; matrix products, arithmetic and copies ran while one was open for 4% of the time, Pallas kernels for 0%

commit v1 on v0

--- a/solution.py
+++ b/solution.py
@@ -1,9 +1,23 @@
+import functools
 import jax
 import jax.numpy as jnp
 from jax import lax
 from jax.sharding import PartitionSpec as P
 
 epsilon = 1e-05
+
+
+def wait_the_values(raw, device_axis):
+    made = []
+    for _ in range(lax.axis_size(device_axis)):
+        made.append(raw)
+    arr_now = jnp.concatenate(
+        lax.all_to_all(jnp.stack(made), axis_name=device_axis, split_axis=0, concat_axis=0), 0
+    )
+    return arr_now
+
+
+return_all_wires = functools.partial(wait_the_values, device_axis="col")
 
 
 def swiglu_grads(hidden_grad, pre_gate, pre_up):
@@ -37,9 +51,7 @@
     )
     summed_grad = lax.psum(partial_grad, "col")
     hidden_piece, gate_piece, up_piece = swiglu_grads(
-        summed_grad,
-        lax.all_gather(pre_gate, "col", axis=0, tiled=True),
-        lax.all_gather(pre_up, "col", axis=0, tiled=True),
+        summed_grad, lax.all_gather(pre_gate, "col", axis=0, tiled=True), return_all_wires(pre_up)
     )
     down_total = jnp.einsum("tf,td->fd", hidden_piece, all_grad, preferred_element_type=jnp.float32)
     gate_total = jnp.einsum("td,tf->df", all_input, gate_piece, preferred_element_type=jnp.float32)

time: 566 us -> 594 us (1.049)
  blocking collectives: 81 us -> 195 us
  waiting for transfers between devices: 394 us -> 306 us
    all_to_all x0 -> x1, blocking collectives: none -> 114 us  [wait_the_values(): lax.all_to_all(jnp.stack(made), axis_name=device_axis, split_axis=0, conc...]
    all_gather x1, waiting for transfers between devices: 49.7 us -> 0.01 us  [local(): lax.all_gather(pre_gate, 'col', axis=0, tiled=True)]
    all_gather x1 -> x0, waiting for transfers between devices: 38.1 us -> none  [local(): lax.all_gather(pre_up, 'col', axis=0, tiled=True)]
  transfers between devices with their start and end apart: 8 -> 7, of which waited for: 6 -> 4; matrix products, arithmetic and copies ran while one was open for 4% -> 4% of each run, Pallas kernels for 0% -> 0%
where the time goes in v1:
time: 594 us
  waiting for transfers between devices  306 us (52%)
  blocking collectives  195 us (33%)
  matrix products  49 us (8%)
  other arithmetic  14.4 us (2%)
  between operations  13.9 us (2%)
  starting transfers between devices  10.9 us (2%)
    psum x1, waiting for transfers between devices, local(): summed_grad = lax.psum(partial_grad, 'col')  178 us
    all_to_all x1, blocking collectives, wait_the_values(): lax.all_to_all(jnp.stack(made), axis_name=device_axis, split_axis=0, conc...  114 us
    reduce_scatter x1, waiting for transfers between devices, local(): lax.psum_scatter(back_rows, 'row', scatter_dimension=0, tiled=True)  75.7 us
    psum x1, blocking collectives, local(): grad_gain = lax.psum(jnp.sum(normed_grad * normed, axis=0), ('row', 'col'))  67.4 us
    all_gather x1, waiting for transfers between devices, local(): lax.all_gather(grid_grad, 'row', axis=0, tiled=True)  44.7 us
    all_to_all x1, blocking collectives, local(): lax.all_to_all(grad_out, 'col', split_axis=1, concat_axis=0, tiled=True)  13.5 us
    convert_element_type x1, other arithmetic, swiglu_grads(): up_grad = (hidden_grad * silu).astype(jnp.bfloat16)  12.5 us
  transfers between devices with their start and end apart: 7, of which 4 were waited for; matrix products, arithmetic and copies ran while one was open for 4% of the time, Pallas kernels for 0%

profile of v1, /device:TPU:1, one launch (start us, length us, event | category | flops | bytes accessed | tf_op | source)
XLA Modules:
  0.0 593.7 jit_solution(18030427107382117201)
XLA Ops:
  7.2 0.0 all-gather.4.cloned.1.call-start
  7.2 13.5 %all_to_all.62 = bf16[8,16,512]{2,0,1:T(8,128)(2,1)} all-to-all(bf16[8,16,512]{2,0,1:T(8,128)(2,1)} %bitcast.31), channel_id=1, replica_groups=mesh['row'=8,'col'=16] {'col'}, dimensions={1} | all-to-all | bytes 262144 | tf_op jit(solution)/shard_map/all_to_all | solution.py:43
  20.7 0.0 all-gather.4.cloned.1.call-update
  20.7 0.0 all-gather.6.cloned.1.call-start
  20.8 0.7 all-gather.6.cloned.1.call-update
  21.5 0.0 all-reduce.2.cloned.1.call-start
  21.5 44.7 %all-gather.4.cloned.1.call-done = bf16[1024,512]{1,0:T(8,128)(2,1)} async-done(((bf16[128,512]{1,0:T(8,128)(2,1)}), bf16[1024,512]{1,0:T(8,128)(2,1)}) %all-gather.4.cloned.1.call-update) | async-done | bytes 1048592 | tf_op jit(solution)/shard_map/all_gather | solution.py:47
  66.2 11.5 %fusion.26 = f32[1024,3584]{1,0:T(8,128)} fusion(bf16[1024,512]{1,0:T(8,128)(2,1)} %all-gather.4.cloned.1.call-done, bf16[3584,512]{1,0:T(8,128)(2,1)} %param.15), kind=kOutput, calls=%fused_computation.36 | convolution fusion | flops 3758096384 | bytes 19398656 | tf_op jit(solution)/shard_map/td,fd->tf/dot_general | solution.py:49
  77.7 0.0 all-reduce.2.cloned.1.call-update
  77.7 0.0 reduce-scatter.2.cloned.1.call-start
  77.8 0.9 copy-done.5
  78.7 0.7 stack.2
  79.4 114.0 %all_to_all.63 = bf16[16,64,3584]{2,1,0:T(8,128)(2,1)} all-to-all(bf16[16,64,3584]{2,1,0:T(8,128)(2,1)S(1)} %stack.2), channel_id=1, replica_groups=mesh['row'=8,'col'=16] {'col'}, dimensions={0} | all-to-all | bytes 14680064 | tf_op jit(solution)/shard_map/all_to_all | solution.py:15
  193.4 178.1 %all-reduce.2.cloned.1.call-done = f32[1024,3584]{1,0:T(8,128)} async-done(((f32[1024,3584]{1,0:T(8,128)}), f32[1024,3584]{1,0:T(8,128)}) %all-reduce.2.cloned.1.call-update) | async-done | bytes 14680080 | tf_op jit(solution)/shard_map/psum | solution.py:52
  371.6 12.5 %multiply_convert_fusion = (bf16[1024,3584]{1,0:T(8,128)(2,1)S(1)}, bf16[1024,3584]{1,0:T(8,128)(2,1)S(1)}) fusion(f32[1024,3584]{1,0:T(8,128)} %all-reduce.2.cloned.1.call-done, bf16[1024,3584]{1,0:T(8,128)(2,1)} %all-gather.6.cloned.1.call-done, bf16[16,64,3584]{2,1,0:T(8,128)(2,1)} %all_to_all.63), kind=kLoop, calls=%fused_computation.13 | loop fusion | flops 55050240 | bytes 44040192 | tf_op jit(solution)/shard_map/convert_element_type | solution.py:29
  384.1 4.0 fusion.27
  388.1 2.0 copy-done.1
  390.1 5.3 convolution_add_fusion
  395.4 75.7 %reduce-scatter.2.cloned.1.call-done = f32[128,512]{1,0:T(8,128)} async-done(((f32[1024,512]{1,0:T(8,128)}), f32[128,512]{1,0:T(8,128)}) %reduce-scatter.2.cloned.1.call-update) | async-done | bytes 262160 | tf_op jit(solution)/shard_map/reduce_scatter | solution.py:66
  471.1 6.5 %all-to-all-start.2 = ((f32[16,8,512]{2,1,0:T(8,128)}), f32[16,8,512]{2,1,0:T(8,128)S(1)}, u32[]{:S(2)}, u32[]{:S(2)}) async-start(f32[16,8,512]{2,1,0:T(8,128)} %bitcast.32), calls=%async_computation.3 | async-start | bytes 524288 | tf_op jit(solution)/shard_map/all_to_all | solution.py:67
  477.6 0.2 fusion.24
  477.8 7.0 %all-to-all-done.2 = f32[16,8,512]{2,1,0:T(8,128)S(1)} async-done(((f32[16,8,512]{2,1,0:T(8,128)}), f32[16,8,512]{2,1,0:T(8,128)S(1)}, u32[]{:S(2)}, u32[]{:S(2)}) %all-to-all-start.2) | async-done | bytes 262176 | tf_op jit(solution)/shard_map/all_to_all | solution.py:67
  484.8 0.9 fusion.22
  485.7 4.0 all-to-all-start.3
  489.8 0.2 all-gather.8.cloned.1.call-start
  490.0 10.3 %fusion.10 = bf16[3584,512]{1,0:T(8,128)(2,1)} fusion(bf16[1024,512]{1,0:T(8,128)(2,1)S(1)} %copy-done.9, bf16[1024,3584]{1,0:T(8,128)(2,1)} %bitcast.26, bf16[1024,3584]{1,0:T(8,128)(2,1)} %all-gather.6.cloned.1.call-done), kind=kOutput, calls=%fused_computation.15 | convolution fusion | flops 3789291520 | bytes 19398656 | tf_op jit(solution)/shard_map/tf,td->fd/dot_general | solution.py:56
  500.4 0.7 copy-done.3
  501.0 0.0 all-gather.8.cloned.1.call-update
  501.1 67.4 %psum.15 = f32[8192]{0:T(1024)} all-reduce(f32[8192]{0:T(1024)S(1)} %get-tuple-element.5), channel_id=1, replica_groups=mesh['row'=8,'col'=16] {'row','col'}, use_global_device_ids=true, to_apply=%region_5.0 | all-reduce | flops 8192 | bytes 65536 | tf_op jit(solution)/shard_map/psum | solution.py:68
  568.5 0.8 fusion.21
  569.3 9.3 %convolution_convert_fusion = bf16[512,3584]{1,0:T(8,128)(2,1)} fusion(bf16[1024,512]{1,0:T(8,128)(2,1)} %all-gather.8.cloned.1.call-done, bf16[1024,3584]{1,0:T(8,128)(2,1)} %copy-done.1), kind=kOutput, calls=%fused_computation.16 | convolution fusion | flops 3759931392 | bytes 12058624 | tf_op jit(solution)/shard_map/td,tf->df/dot_general | solution.py:58
  578.6 8.5 %convolution_convert_fusion.1 = bf16[512,3584]{1,0:T(8,128)(2,1)} fusion(bf16[1024,512]{1,0:T(8,128)(2,1)S(1)} %copy-done.10, bf16[1024,3584]{1,0:T(8,128)(2,1)} %copy-done), kind=kOutput, calls=%fused_computation.17 | convolution fusion | flops 3759931392 | bytes 12058624 | tf_op jit(solution)/shard_map/td,tf->df/dot_general | solution.py:57
  (25 shorter events, 0.1 us)
Async XLA Ops:
  7.2 59.0 %all-gather.4.cloned.1.call-start = ((), (), s32[]{:S(2)}) async-start(), calls=%async_computation.5 | async-start | bytes 1179648 | tf_op jit(solution)/shard_map/all_gather | solution.py:47
  20.7 172.7 %all-gather.6.cloned.1.call-start = ((), (), s32[]{:S(2)}) async-start(), calls=%async_computation.7 | async-start | bytes 7798784 | tf_op jit(solution)/shard_map/all_gather | solution.py:54
  21.5 350.1 %all-reduce.2.cloned.1.call-start = ((), (), s32[]{:S(2)}) async-start(), calls=%async_computation.6 | async-start | bytes 29360128 | tf_op jit(solution)/shard_map/psum | solution.py:52
  77.7 1.0 copy-start.5
  77.7 393.4 %reduce-scatter.2.cloned.1.call-start = ((), (), s32[]{:S(2)}) async-start(), calls=%async_computation.8 | async-start | bytes 2359296 | tf_op jit(solution)/shard_map/reduce_scatter | solution.py:66
  371.6 12.5 %copy-start.7 = (bf16[512,3584]{1,0:T(8,128)(2,1)S(1)}, bf16[512,3584]{1,0:T(8,128)(2,1)}, u32[]{:S(2)}) copy-start(bf16[512,3584]{1,0:T(8,128)(2,1)} %param.13) | copy-start | bytes 11010052
  384.1 4.0 copy-start
  384.1 6.0 %copy-start.1 = (bf16[1024,3584]{1,0:T(8,128)(2,1)}, bf16[1024,3584]{1,0:T(8,128)(2,1)S(1)}, u32[]{:S(2)}) copy-start(bf16[1024,3584]{1,0:T(8,128)(2,1)S(1)} %get-tuple-element.7) | copy-start | bytes 22020100
  384.1 6.0 %copy-start.8 = (bf16[512,3584]{1,0:T(8,128)(2,1)S(1)}, bf16[512,3584]{1,0:T(8,128)(2,1)}, u32[]{:S(2)}) copy-start(bf16[512,3584]{1,0:T(8,128)(2,1)} %param.14) | copy-start | bytes 11010052
  390.1 87.6 %copy-start.2 = (bf16[8,8192]{1,0:T(8,128)(2,1)S(1)}, bf16[8,8192]{1,0:T(8,128)(2,1)}, u32[]{:S(2)}) copy-start(bf16[8,8192]{1,0:T(8,128)(2,1)} %param.8) | copy-start | bytes 393220
  390.1 94.8 %copy-start.6 = (f32[8192]{0:T(1024)S(1)}, f32[8192]{0:T(1024)}, u32[]{:S(2)}) copy-start(f32[8192]{0:T(1024)} %param.9) | copy-start | bytes 98308
  390.1 100.0 %copy-start.9 = (bf16[1024,512]{1,0:T(8,128)(2,1)S(1)}, bf16[1024,512]{1,0:T(8,128)(2,1)}, u32[]{:S(2)}) copy-start(bf16[1024,512]{1,0:T(8,128)(2,1)} %all-gather.4.cloned.1.call-done) | copy-start | bytes 3145732
  471.1 13.7 %all-to-all-start.2 = ((f32[16,8,512]{2,1,0:T(8,128)}), f32[16,8,512]{2,1,0:T(8,128)S(1)}, u32[]{:S(2)}, u32[]{:S(2)}) async-start(f32[16,8,512]{2,1,0:T(8,128)} %bitcast.32), calls=%async_computation.3 | async-start | bytes 524288 | tf_op jit(solution)/shard_map/all_to_all | solution.py:67
  485.7 14.6 %all-to-all-start.3 = ((bf16[8,16,512]{2,0,1:T(8,128)(2,1)}), bf16[8,16,512]{2,0,1:T(8,128)(2,1)S(1)}, u32[]{:S(2)}, u32[]{:S(2)}) async-start(bf16[8,16,512]{2,0,1:T(8,128)(2,1)} %bitcast.8), calls=%async_computation.4 | async-start | bytes 262144 | tf_op jit(solution)/shard_map/all_to_all | solution.py:42
  489.8 79.5 %all-gather.8.cloned.1.call-start = ((), (), s32[]{:S(2)}) async-start(), calls=%async_computation.9 | async-start | bytes 1179648 | tf_op jit(solution)/shard_map/all_gather | solution.py:46
  490.0 78.5 %copy-start.4 = (bf16[8,8192]{1,0:T(8,128)(2,1)S(1)}, bf16[8,8192]{1,0:T(8,128)(2,1)}, u32[]{:S(2)}) copy-start(bf16[8,8192]{1,0:T(8,128)(2,1)} %param.10) | copy-start | bytes 393220
  500.4 0.7 copy-start.3
  569.3 9.3 %copy-start.10 = (bf16[1024,512]{1,0:T(8,128)(2,1)S(1)}, bf16[1024,512]{1,0:T(8,128)(2,1)}, u32[]{:S(2)}) copy-start(bf16[1024,512]{1,0:T(8,128)(2,1)} %all-gather.8.cloned.1.call-done) | copy-start | bytes 3145732
Sparse Core Ops, SparseCore 0:
  20.8 45.2 all-gather.3
  67.9 125.1 all-gather.5
  195.6 175.9 all-reduce.1
  395.5 75.5 reduce-scatter.1
  501.2 45.1 all-gather.7
